TPU v7x, 512 devices: a whole 4x8x8 slice. The times are simulated.
512 devices in a mesh: dp: 32 (over x, z_lo, core), ctx: 16 (over z_hi, y).
Axes of the slice: x: 4, y: 8, z: 8 (z_hi: 2, z_lo: 4; z = z_hi * 4 + z_lo), core: 2. Of those that a mesh axis runs over, the one named last changes fastest.
Arguments:
- queries: bfloat16 [32, 16, 128, 2048], P('dp', 'ctx'), may hold values from -2.5 to 2.5
- rotated_key_rows: bfloat16 [32, 16, 128, 512], P('dp', 'ctx'), may hold values from -2.5 to 2.5
- values: bfloat16 [32, 16, 128, 512], P('dp', 'ctx'), may hold values from -6 to 6
- cotangent: bfloat16 [32, 16, 128, 2048], P('dp', 'ctx'), may hold values from -6 to 6
- hidden: bfloat16 [32, 16, 128, 4096], P('dp', 'ctx'), may hold values from -6 to 6
- adapter_down_weight: bfloat16 [4096, 16], replicated, may hold values from -0.09375 to 0.09375
- adapter_up_weight: bfloat16 [16, 512], replicated, may hold values from -1.5 to 1.5
- segment_text_length: int32 [32, 16], P('dp', 'ctx'), may hold values from 19 to 78, as said below
Outputs:
- grad_queries: bfloat16 [32, 16, 128, 2048], P('dp', 'ctx')
- grad_keys: bfloat16 [32, 16, 128, 512], P('dp', 'ctx')
- grad_values: bfloat16 [32, 16, 128, 512], P('dp', 'ctx')
- grad_down: float32 [4096, 16], replicated
- grad_up: float32 [16, 512], replicated
Inputs may be any that keep to these rules, and one draw needn't show every extreme that they name: `segment_text_length`: every log has a segment with exactly 78 text tokens and another with the fewest.
All inputs are finite; a program needn't handle non-finite values.
Results may differ from a plain program's by a relative error of at most 0.0019.
The roundings to bfloat16 on the way count: a program that leaves them out, or rounds other values in their place, can miss the bound.
Values may be sent and summed in bfloat16 or wider, within the bound.
No kernel may reach another device: no remote copies, remote signals or barrier semaphores. Data moves between devices by JAX's collectives and lax.ppermute only.
A program may use at most 64 MiB of HBM per device.

v0:
```python
import math
import jax
import jax.numpy as jnp
from jax import lax
from jax.sharding import PartitionSpec as P

HEAD_SIZE = 128
SUMM = 50
adapter_scale = 2.0


def group_grads(query_group, key_group, value_group, cot_group, key_mask):
    softmax_scale = 1.0 / math.sqrt(HEAD_SIZE)
    scores = (
        jnp.einsum("tgd,md->gtm", query_group, key_group, preferred_element_type=jnp.float32)
        * softmax_scale
    )
    unnorm = jnp.exp(jnp.where(key_mask[None], scores, -jnp.inf))
    attend = unnorm / jnp.sum(unnorm, -1, keepdims=True)
    attend_grad = jnp.einsum(
        "tgd,md->gtm", cot_group, value_group, preferred_element_type=jnp.float32
    )
    row_dot = jnp.sum(attend * attend_grad, -1, keepdims=True)
    dscore = (attend * (attend_grad - row_dot)).astype(jnp.bfloat16)
    attend_low = attend.astype(jnp.bfloat16)
    query_grad = (
        jnp.einsum("gtm,md->tgd", dscore, key_group, preferred_element_type=jnp.float32)
        * softmax_scale
    )
    key_grad = (
        jnp.einsum("gtm,tgd->md", dscore, query_group, preferred_element_type=jnp.float32)
        * softmax_scale
    )
    value_grad = jnp.einsum(
        "gtm,tgd->md", attend_low, cot_group, preferred_element_type=jnp.float32
    )
    return (query_grad, key_grad, value_grad)


def adapter_terms(hidden_piece, low_rank_piece, value_piece, adapter_up_weight):
    contract = (((0,), (0,)), ((), ()))
    backward_step = lax.dot_general(
        value_piece, adapter_up_weight, (((1,), (1,)), ((), ())), preferred_element_type=jnp.float32
    ).astype(jnp.bfloat16)
    down_part = lax.dot_general(
        hidden_piece, backward_step, contract, preferred_element_type=jnp.float32
    )
    up_part = lax.dot_general(
        low_rank_piece, value_piece, contract, preferred_element_type=jnp.float32
    )
    return (down_part, up_part)


def per_device(
    queries,
    rotated_key_rows,
    values,
    cotangent,
    hidden,
    adapter_down_weight,
    adapter_up_weight,
    segment_text_length,
):
    query_rows = queries[0, 0]
    key_local = rotated_key_rows[0, 0]
    value_local = values[0, 0]
    cot_rows = cotangent[0, 0]
    hidden_row_block = hidden[0, 0]
    length = segment_text_length[0, 0]
    position = lax.axis_index("ctx")
    segment_list = lax.axis_size("ctx")
    log_batch = lax.axis_size("dp")
    tokens = query_rows.shape[0]
    width = key_local.shape[1]
    kv_heads = width // HEAD_SIZE
    groups = query_rows.shape[1] // width
    live = length + SUMM
    rows = jnp.arange(tokens)
    cot_rows = jnp.where((rows < live)[:, None], cot_rows, jnp.zeros_like(cot_rows))
    own_keys = lax.dynamic_slice_in_dim(key_local, length, SUMM, 0)
    own_values = lax.dynamic_slice_in_dim(value_local, length, SUMM, 0)
    memory_keys, memory_values = (
        lax.all_gather(own_keys, "ctx", axis=0, tiled=True),
        lax.all_gather(own_values, "ctx", axis=0, tiled=True),
    )
    count = memory_keys.shape[0]
    memory_owner = jnp.arange(count) // SUMM
    local_mask = (rows[None, :] <= rows[:, None]) & (rows[None, :] < live)
    memory_mask = jnp.broadcast_to((memory_owner < position)[None, :], (tokens, count))
    key_mask = jnp.concatenate([memory_mask, local_mask], axis=1)
    all_keys = jnp.concatenate([memory_keys, key_local], 0)
    all_values = jnp.concatenate([memory_values, value_local], 0)
    query_parts, key_parts, value_parts = ([], [], [])
    for group in range(kv_heads):
        qcols = slice(group * groups * HEAD_SIZE, (group + 1) * groups * HEAD_SIZE)
        kcols = slice(group * HEAD_SIZE, (group + 1) * HEAD_SIZE)
        query_grad, key_grad, value_grad = group_grads(
            query_rows[:, qcols].reshape(tokens, groups, HEAD_SIZE),
            all_keys[:, kcols],
            all_values[:, kcols],
            cot_rows[:, qcols].reshape(tokens, groups, HEAD_SIZE),
            key_mask,
        )
        query_parts.append(query_grad.reshape(tokens, groups * HEAD_SIZE))
        key_parts.append(key_grad)
        value_parts.append(value_grad)
    query_out = jnp.concatenate(query_parts, 1).astype(jnp.bfloat16)
    key_grad = jnp.concatenate(key_parts, 1)
    value_grad = jnp.concatenate(value_parts, 1)
    memory_key_grad, local_key = (key_grad[:count], key_grad[count:])
    memory_value_grad, local_value = (value_grad[:count], value_grad[count:])
    back_key, back_value = (
        lax.psum_scatter(memory_key_grad, "ctx", scatter_dimension=0, tiled=True),
        lax.psum_scatter(memory_value_grad, "ctx", scatter_dimension=0, tiled=True),
    )
    key_out = (
        local_key + lax.dynamic_update_slice_in_dim(jnp.zeros_like(local_key), back_key, length, 0)
    ).astype(jnp.bfloat16)
    value_result = (
        local_value
        + lax.dynamic_update_slice_in_dim(jnp.zeros_like(local_value), back_value, length, 0)
    ).astype(jnp.bfloat16)
    low_rank_rows = jnp.dot(
        hidden_row_block, adapter_down_weight, preferred_element_type=jnp.float32
    ).astype(jnp.bfloat16)
    down_sum, up_sum = lax.psum(
        adapter_terms(hidden_row_block, low_rank_rows, value_result, adapter_up_weight),
        ("dp", "ctx"),
    )
    adapter_factor = adapter_scale / (log_batch * segment_list)
    return (
        query_out[None, None],
        key_out[None, None],
        value_result[None, None],
        down_sum * adapter_factor,
        up_sum * adapter_factor,
    )


def solution(mesh):
    placed = (
        P("dp", "ctx", None, None),
        P("dp", "ctx", None, None),
        P("dp", "ctx", None, None),
        P("dp", "ctx", None, None),
        P("dp", "ctx", None, None),
        P(),
        P(),
        P("dp", "ctx"),
    )
    return jax.shard_map(
        per_device,
        mesh=mesh,
        in_specs=placed,
        out_specs=(
            P("dp", "ctx", None, None),
            P("dp", "ctx", None, None),
            P("dp", "ctx", None, None),
            P(),
            P(),
        ),
        check_vma=False,
    )
```

profile of v0, /device:TPU:23, one launch (start us, length us, event | category | flops | bytes accessed | tf_op | source)
XLA Modules:
  0.0 690.2 jit_solution(10573385685993678899)
XLA Ops:
  9.1 0.9 constant_dynamic-slice_fusion
  10.0 1.3 copy.64
  12.5 56.8 %all-gather.1 = bf16[1,1,800,512]{3,1,0,2:T(2,128)(2,1)S(1)} all-gather(bf16[1,1,50,512]{3,1,0,2:T(2,128)(2,1)S(1)} %copy.106), channel_id=3, replica_groups=mesh['dp'=32,'ctx'=16] {'ctx'}, dimensions={2}, use_global_device_ids=true | all-gather | bytes 870400 | tf_op jit(solution)/shard_map/all_gather | solution.py:84
  69.5 58.1 %all-gather = bf16[1,1,800,512]{3,1,0,2:T(2,128)(2,1)S(1)} all-gather(bf16[1,1,50,512]{3,1,0,2:T(2,128)(2,1)S(1)} %copy.105), channel_id=2, replica_groups=mesh['dp'=32,'ctx'=16] {'ctx'}, dimensions={2}, use_global_device_ids=true | all-gather | bytes 870400 | tf_op jit(solution)/shard_map/all_gather | solution.py:83
  127.8 1.7 fusion.48
  129.5 1.6 fusion.52
  131.1 1.7 fusion.61
  132.8 1.6 fusion.44
  134.7 3.7 fusion.6
  138.4 2.1 convolution_bitcast_fusion.2
  140.5 1.8 fusion.8
  142.4 1.0 copy-done.1
  143.4 1.2 fusion.19
  144.6 4.1 fusion.2
  148.7 2.9 convolution_bitcast_fusion.1
  151.6 1.8 fusion.4
  153.4 1.2 fusion.18
  154.6 4.3 fusion.10
  158.9 2.9 convolution_bitcast_fusion.3
  161.8 1.8 fusion.12
  163.7 0.9 copy-done.2
  164.6 1.2 fusion.20
  165.8 4.2 fusion.14
  170.0 2.1 convolution_bitcast_fusion.4
  172.2 2.0 fusion.16
  174.2 1.0 copy-done.4
  175.7 1.9 pad_maximum_fusion
  177.5 77.3 %fusion.89 = (f32[56,512]{1,0:T(8,128)}, f32[56,512]{1,0:T(8,128)}) fusion(f32[800,512]{1,0:T(8,128)} %get-tuple-element.26, f32[800,512]{1,0:T(8,128)} %get-tuple-element.25), kind=kCustom, calls=%all-reduce-scatter.2 | all-reduce-scatter fusion | flops 917505 | bytes 3508224
  254.8 2.0 collective-permute-start.2
  256.9 1.5 slice.107
  258.4 1.9 collective-permute-start.3
  260.3 1.9 collective-permute-start
  262.3 1.5 slice.106
  263.8 12.0 %collective-permute-start.1 = (f32[34,512]{1,0:T(8,128)}, f32[34,512]{1,0:T(8,128)}, u32[]{:S(2)}, u32[]{:S(2)}) collective-permute-start(f32[34,512]{1,0:T(8,128)} %slice.106), channel_id=1, source_target_pairs={{0,2},{1,3},{2,4},{3,5},{4,6},{5,7},{6,8},{7,9},{8,10},{9,11},{10,... | collective-permute-start | bytes 208904
  275.7 2.2 fusion.24
  277.9 1.0 fusion.25
  279.0 1.0 fusion.23
  280.0 1.0 fusion.22
  282.8 1.0 copy.76
  283.8 1.7 copy.75
  285.5 1.3 dynamic-slice.10
  287.4 1.8 pad_maximum_fusion.6
  289.3 2.8 concatenate.44
  293.7 2.8 concatenate.45
  298.6 116.7 %psum.15 = f32[16,512]{1,0:T(8,128)S(1)} all-reduce(f32[16,512]{1,0:T(8,128)S(1)} %fusion.26), channel_id=1, replica_groups=mesh['dp'=32,'ctx'=16] {'dp','ctx'}, use_global_device_ids=true, to_apply=%region_11.12 | all-reduce | flops 8192 | bytes 65536 | tf_op jit(solution)/shard_map/psum | solution.py:126
  415.3 1.2 convolution_bitcast_fusion
  417.1 264.6 %all-reduce.7.cloned.1.call-done = f32[4096,16]{0,1:T(8,128)} async-done(((f32[4096,16]{0,1:T(8,128)}), f32[4096,16]{0,1:T(8,128)}) %all-reduce.7.cloned.1.call-update) | async-done | bytes 262160 | tf_op jit(solution)/shard_map/psum | solution.py:126
  681.7 1.7 broadcast_multiply_fusion
  (115 shorter events, 9.5 us)
Async XLA Ops:
  7.2 290.9 %copy-start = (bf16[1,1,128,4096]{3,2,1,0:T(8,128)(2,1)S(1)}, bf16[1,1,128,4096]{3,2,1,0:T(8,128)(2,1)}, u32[]{:S(2)}) copy-start(bf16[1,1,128,4096]{3,2,1,0:T(8,128)(2,1)} %param.12) | copy-start | bytes 3145732
  7.2 4.9 copy-start.31
  7.2 674.5 %all-reduce.7.cloned.1.call-start = ((), (), s32[]{:S(2)}) async-start(), calls=%async_computation | async-start | bytes 524288 | tf_op jit(solution)/shard_map/psum | solution.py:126
  12.1 132.5 %copy-start.34 = (bf16[128,512]{0,1:T(8,128)(2,1)}, bf16[128,512]{0,1:T(8,128)(2,1)S(1)}, u32[]{:S(2)}) copy-start(bf16[128,512]{0,1:T(8,128)(2,1)S(1)} %get-tuple-element.14) | copy-start | bytes 393220
  12.5 117.0 %copy-start.26 = (bf16[128,512]{0,1:T(8,128)(2,1)}, bf16[128,512]{0,1:T(8,128)(2,1)S(1)}, u32[]{:S(2)}) copy-start(bf16[128,512]{0,1:T(8,128)(2,1)S(1)} %get-tuple-element.12) | copy-start | bytes 393220
  69.5 58.3 %copy-start.24 = (bf16[1,1,128,512]{3,2,1,0:T(8,128)(2,1)S(1)}, bf16[1,1,128,512]{3,2,1,0:T(8,128)(2,1)}, u32[]{:S(2)}) copy-start(bf16[1,1,128,512]{3,2,1,0:T(8,128)(2,1)} %param.10) | copy-start | bytes 393220
  132.8 1.8 copy-start.25
  134.7 9.9 %copy-start.37 = (pred[128,928]{0,1:T(8,128)(4,1)}, pred[128,928]{0,1:T(8,128)(4,1)S(1)}, u32[]{:S(2)}) copy-start(pred[128,928]{0,1:T(8,128)(4,1)S(1)} %pad_add_fusion) | copy-start | bytes 356356
  134.7 9.9 %copy-start.27 = (bf16[928,128,1]{1,0,2:T(8,128)(2,1)}, bf16[928,128,1]{1,0,2:T(8,128)(2,1)S(1)}, u32[]{:S(2)}) copy-start(bf16[928,128,1]{1,0,2:T(8,128)(2,1)S(1)} %fusion.64) | copy-start | bytes 712708
  138.4 2.1 copy-start.9
  142.3 1.0 copy-start.1
  148.7 2.9 copy-start.8
  148.7 2.9 copy-start.40
  151.6 1.8 copy-start.35
  158.9 2.9 copy-start.7
  158.9 2.9 copy-start.41
  161.8 2.8 copy-start.33
  163.7 0.9 copy-start.2
  170.0 2.1 copy-start.6
  170.0 2.1 copy-start.39
  172.1 3.5 copy-start.14
  172.1 3.1 copy-start.32
  172.1 3.5 copy-start.10
  172.1 3.5 copy-start.12
  172.2 3.5 copy-start.16
  172.2 3.5 copy-start.18
  172.2 3.5 copy-start.20
  174.2 1.0 copy-start.4
  175.6 1.9 copy-start.22
  254.8 23.1 %copy-start.28 = (bf16[928,128,1]{1,0,2:T(8,128)(2,1)S(1)}, bf16[928,128,1]{1,0,2:T(8,128)(2,1)}, u32[]{:S(2)}) copy-start(bf16[928,128,1]{1,0,2:T(8,128)(2,1)} %copy-done.27) | copy-start | bytes 712708
  254.8 24.1 %copy-start.3 = (bf16[4,128,928]{1,2,0:T(8,128)(2,1)S(1)}, bf16[4,128,928]{1,2,0:T(8,128)(2,1)}, u32[]{:S(2)}) copy-start(bf16[4,128,928]{1,2,0:T(8,128)(2,1)} %copy-done.2) | copy-start | bytes 2850820
  254.8 38.9 %collective-permute-start.2 = (f32[56,512]{1,0:T(8,128)}, f32[56,512]{1,0:T(8,128)}, u32[]{:S(2)}, u32[]{:S(2)}) collective-permute-start(f32[56,512]{1,0:T(8,128)} %get-tuple-element.8), channel_id=1, source_target_pairs={{0,1},{1,2},{2,3},{3,4},{4,5},{5,6},{6,7},{7,8},{8,9},{9,10},{10,1... | collective-permute-start | bytes 344072
  258.4 35.3 %collective-permute-start.3 = (f32[34,512]{1,0:T(8,128)}, f32[34,512]{1,0:T(8,128)}, u32[]{:S(2)}, u32[]{:S(2)}) collective-permute-start(f32[34,512]{1,0:T(8,128)} %slice.107), channel_id=1, source_target_pairs={{0,2},{1,3},{2,4},{3,5},{4,6},{5,7},{6,8},{7,9},{8,10},{9,11},{10,... | collective-permute-start | bytes 208904
  260.3 28.9 %collective-permute-start = (f32[56,512]{1,0:T(8,128)}, f32[56,512]{1,0:T(8,128)}, u32[]{:S(2)}, u32[]{:S(2)}) collective-permute-start(f32[56,512]{1,0:T(8,128)} %get-tuple-element.7), channel_id=1, source_target_pairs={{0,1},{1,2},{2,3},{3,4},{4,5},{5,6},{6,7},{7,8},{8,9},{9,10},{10,1... | collective-permute-start | bytes 344072
  263.8 25.5 %collective-permute-start.1 = (f32[34,512]{1,0:T(8,128)}, f32[34,512]{1,0:T(8,128)}, u32[]{:S(2)}, u32[]{:S(2)}) collective-permute-start(f32[34,512]{1,0:T(8,128)} %slice.106), channel_id=1, source_target_pairs={{0,2},{1,3},{2,4},{3,5},{4,6},{5,7},{6,8},{7,9},{8,10},{9,11},{10,... | collective-permute-start | bytes 208904
  277.9 2.0 copy-start.5
  278.9 2.0 copy-start.17
  278.9 2.0 copy-start.19
  278.9 2.0 copy-start.21
  278.9 2.0 copy-start.23
  281.0 0.9 copy-start.29
  281.0 1.7 copy-start.30
  281.0 8.2 %copy-start.11 = (f32[928,128]{1,0:T(8,128)S(1)}, f32[928,128]{1,0:T(8,128)}, u32[]{:S(2)}) copy-start(f32[928,128]{1,0:T(8,128)} %convolution_bitcast_fusion.1) | copy-start | bytes 1425412
  281.0 8.2 %copy-start.13 = (f32[928,128]{1,0:T(8,128)S(1)}, f32[928,128]{1,0:T(8,128)}, u32[]{:S(2)}) copy-start(f32[928,128]{1,0:T(8,128)} %convolution_bitcast_fusion.3) | copy-start | bytes 1425412
  281.0 8.2 %copy-start.15 = (f32[928,128]{1,0:T(8,128)S(1)}, f32[928,128]{1,0:T(8,128)}, u32[]{:S(2)}) copy-start(f32[928,128]{1,0:T(8,128)} %copy-done.14) | copy-start | bytes 1425412
  289.2 8.9 %copy-start.36 = (bf16[4096,16]{0,1:T(8,128)(2,1)S(1)}, bf16[4096,16]{0,1:T(8,128)(2,1)}, u32[]{:S(2)}) copy-start(bf16[4096,16]{0,1:T(8,128)(2,1)} %param.13) | copy-start | bytes 393220
  292.2 123.2 %copy-start.38 = (bf16[16,512]{1,0:T(8,128)(2,1)S(1)}, bf16[16,512]{1,0:T(8,128)(2,1)}, u32[]{:S(2)}) copy-start(bf16[16,512]{1,0:T(8,128)(2,1)} %param.14) | copy-start | bytes 49156
Sparse Core Ops, SparseCore 0:
  416.6 265.0 all-reduce.6
where the time goes:
time: 691 us; the launch traced here: 690 us
  blocking collectives  309 us (45%)
  waiting for transfers between devices  265 us (38%)
  matrix products  43.7 us (6%)
  local copies, waits for them, and re-layouts  23.8 us (3%)
  starting transfers between devices  17.9 us (3%)
  between operations  16 us (2%)
  other arithmetic  15.3 us (2%)
    psum x1, waiting for transfers between devices, per_device(): lax.psum(adapter_terms(hidden_row_block, low_rank_rows, value_result, ada...  265 us
    psum x1, blocking collectives, per_device(): lax.psum(adapter_terms(hidden_row_block, low_rank_rows, value_result, ada...  117 us
    unnamed x1, blocking collectives  77.3 us
    all_gather x1, blocking collectives, per_device(): lax.all_gather(own_keys, 'ctx', axis=0, tiled=True)  58.1 us
    all_gather x1, blocking collectives, per_device(): lax.all_gather(own_values, 'ctx', axis=0, tiled=True)  56.8 us
    unnamed x4, starting transfers between devices  17.8 us
    div x4, matrix products, group_grads(): attend = unnorm / jnp.sum(unnorm, -1, keepdims=True)  16.4 us
    unnamed x95, local copies, waits for them, and re-layouts  16.1 us
  transfers between devices with their start and end apart: 5, of which 1 were waited for; matrix products, arithmetic and copies ran while one was open for 3% of the time, Pallas kernels for 0%

commit v1 on v0

--- a/solution.py
+++ b/solution.py
@@ -80,7 +80,9 @@
     own_keys = lax.dynamic_slice_in_dim(key_local, length, SUMM, 0)
     own_values = lax.dynamic_slice_in_dim(value_local, length, SUMM, 0)
     memory_keys, memory_values = (
-        lax.all_gather(own_keys, "ctx", axis=0, tiled=True),
+        jnp.concatenate(
+            lax.all_to_all(jnp.stack([own_keys] * lax.axis_size("ctx")), "ctx", 0, 0), axis=0
+        ),
         lax.all_gather(own_values, "ctx", axis=0, tiled=True),
     )
     count = memory_keys.shape[0]

time: 691 us -> 653 us (0.945)
  blocking collectives: 309 us -> 243 us
  starting transfers between devices: 17.9 us -> 51.1 us
    all_gather x1 -> x0, blocking collectives: 58.1 us -> none  [per_device(): lax.all_gather(own_keys, 'ctx', axis=0, tiled=True)]
    unnamed x4, starting transfers between devices: 17.8 us -> 35.8 us
    all_to_all x0 -> x1, starting transfers between devices: none -> 15.3 us  [per_device(): lax.all_to_all(jnp.stack([own_keys] * lax.axis_size('ctx')), 'ctx', 0, 0)]
    psum x1, blocking collectives: 117 us -> 103 us  [per_device(): lax.psum(adapter_terms(hidden_row_block, low_rank_rows, value_result, ada...]
    all_gather x1, blocking collectives: 56.8 us -> 67.9 us  [per_device(): lax.all_gather(own_values, 'ctx', axis=0, tiled=True)]
    unnamed x95 -> x83, local copies, waits for them, and re-layouts: 16.1 us -> 11.7 us
  transfers between devices with their start and end apart: 5 -> 6, of which waited for: 1 -> 2; matrix products, arithmetic and copies ran while one was open for 3% -> 3% of each run, Pallas kernels for 0% -> 0%
where the time goes in v1:
time: 653 us; the launch traced here: 652 us
  waiting for transfers between devices  264 us (40%)
  blocking collectives  243 us (37%)
  starting transfers between devices  51.1 us (8%)
  matrix products  40 us (6%)
  local copies, waits for them, and re-layouts  20.4 us (3%)
  other arithmetic  16.2 us (2%)
  between operations  16 us (2%)
    psum x1, waiting for transfers between devices, per_device(): lax.psum(adapter_terms(hidden_row_block, low_rank_rows, value_result, ada...  263 us
    psum x1, blocking collectives, per_device(): lax.psum(adapter_terms(hidden_row_block, low_rank_rows, value_result, ada...  103 us
    unnamed x1, blocking collectives  72.3 us
    all_gather x1, blocking collectives, per_device(): lax.all_gather(own_values, 'ctx', axis=0, tiled=True)  67.9 us
    unnamed x4, starting transfers between devices  35.8 us
    all_to_all x1, starting transfers between devices, per_device(): lax.all_to_all(jnp.stack([own_keys] * lax.axis_size('ctx')), 'ctx', 0, 0)  15.3 us
    div x4, matrix products, group_grads(): attend = unnorm / jnp.sum(unnorm, -1, keepdims=True)  14.7 us
  transfers between devices with their start and end apart: 6, of which 2 were waited for; matrix products, arithmetic and copies ran while one was open for 3% of the time, Pallas kernels for 0%

profile of v1, /device:TPU:23, one launch (start us, length us, event | category | flops | bytes accessed | tf_op | source)
XLA Modules:
  0.0 651.7 jit_solution(14758997393797035077)
XLA Ops:
  8.0 0.9 dynamic-slice_bitcast_fusion
  8.8 1.1 stack.5
  9.9 15.3 %all-to-all-start = ((bf16[16,50,512]{2,1,0:T(8,128)(2,1)}), bf16[16,50,512]{2,1,0:T(8,128)(2,1)S(1)}, u32[]{:S(2)}, u32[]{:S(2)}) async-start(bf16[16,50,512]{2,1,0:T(8,128)(2,1)} %stack.5), calls=%async_computation | async-start | bytes 1835008 | tf_op jit(solution)/shard_map/all_to_all | solution.py:84
  26.7 1.3 copy.65
  28.0 67.9 %all-gather = bf16[1,1,800,512]{3,1,0,2:T(2,128)(2,1)S(1)} all-gather(bf16[1,1,50,512]{3,1,0,2:T(2,128)(2,1)S(1)} %copy.102), channel_id=2, replica_groups=mesh['dp'=32,'ctx'=16] {'ctx'}, dimensions={2}, use_global_device_ids=true | all-gather | bytes 870400 | tf_op jit(solution)/shard_map/all_gather | solution.py:86
  96.2 1.3 dynamic-slice.10
  99.0 1.7 fusion.48
  100.7 1.6 fusion.52
  102.3 1.7 fusion.61
  104.0 1.6 fusion.44
  106.6 3.7 fusion.6
  110.3 2.1 convolution_bitcast_fusion.2
  112.4 1.8 fusion.8
  114.2 1.0 fusion.24
  115.6 3.8 fusion.2
  119.4 2.9 convolution_bitcast_fusion.1
  122.3 1.8 fusion.4
  124.2 1.0 fusion.25
  125.2 1.2 fusion.18
  126.3 3.7 fusion.10
  130.0 2.9 convolution_bitcast_fusion.3
  132.9 1.8 fusion.12
  134.7 1.0 fusion.23
  135.7 1.2 fusion.20
  136.9 3.6 fusion.14
  140.5 2.1 convolution_bitcast_fusion.4
  142.6 2.0 fusion.16
  144.6 1.0 fusion.22
  146.8 2.4 pad_maximum_fusion
  149.2 72.3 %fusion.89 = (f32[56,512]{1,0:T(8,128)}, f32[56,512]{1,0:T(8,128)S(1)}) fusion(f32[800,512]{1,0:T(8,128)} %get-tuple-element.26, f32[800,512]{1,0:T(8,128)S(1)} %get-tuple-element.25), kind=kCustom, calls=%all-reduce-scatter.2 | all-reduce-scatter fusion | flops 917505 | bytes 3508224
  221.5 1.6 slice.106
  223.1 2.1 collective-permute-start
  225.8 1.9 collective-permute-start.2
  227.8 1.0 copy.75
  228.8 1.0 copy.76
  229.8 1.0 copy.74
  230.8 1.0 copy.73
  231.9 12.6 %collective-permute-start.3 = (f32[34,512]{1,0:T(8,128)}, f32[34,512]{1,0:T(8,128)}, u32[]{:S(2)}, u32[]{:S(2)}) collective-permute-start(f32[34,512]{1,0:T(8,128)} %slice.107), channel_id=1, source_target_pairs={{0,2},{1,3},{2,4},{3,5},{4,6},{5,7},{6,8},{7,9},{8,10},{9,11},{10,... | collective-permute-start | bytes 208904
  244.5 19.1 %collective-permute-start.1 = (f32[34,512]{1,0:T(8,128)}, f32[34,512]{1,0:T(8,128)S(1)}, u32[]{:S(2)}, u32[]{:S(2)}) collective-permute-start(f32[34,512]{1,0:T(8,128)} %slice.106), channel_id=1, source_target_pairs={{0,2},{1,3},{2,4},{3,5},{4,6},{5,7},{6,8},{7,9},{8,10},{9,11},{10,... | collective-permute-start | bytes 208904
  263.6 0.8 pad_maximum_fusion.6
  264.5 0.9 pad_maximum_fusion.7
  265.4 0.9 collective-permute-done.1
  266.9 2.0 concatenate.44
  270.5 2.0 concatenate.45
  274.6 103.3 %psum.15 = f32[16,512]{1,0:T(8,128)S(1)} all-reduce(f32[16,512]{1,0:T(8,128)S(1)} %fusion.26), channel_id=1, replica_groups=mesh['dp'=32,'ctx'=16] {'dp','ctx'}, use_global_device_ids=true, to_apply=%region_11.12 | all-reduce | flops 8192 | bytes 65536 | tf_op jit(solution)/shard_map/psum | solution.py:128
  377.9 1.2 convolution_bitcast_fusion
  379.7 263.5 %all-reduce.7.cloned.1.call-done = f32[4096,16]{0,1:T(8,128)} async-done(((f32[4096,16]{0,1:T(8,128)}), f32[4096,16]{0,1:T(8,128)}) %all-reduce.7.cloned.1.call-update) | async-done | bytes 262160 | tf_op jit(solution)/shard_map/psum | solution.py:128
  643.2 1.7 broadcast_multiply_fusion
  (106 shorter events, 10.6 us)
Async XLA Ops:
  7.2 266.9 %copy-start = (bf16[1,1,128,4096]{3,2,1,0:T(8,128)(2,1)S(1)}, bf16[1,1,128,4096]{3,2,1,0:T(8,128)(2,1)}, u32[]{:S(2)}) copy-start(bf16[1,1,128,4096]{3,2,1,0:T(8,128)(2,1)} %param.12) | copy-start | bytes 3145732
  7.2 18.3 %copy-start.13 = (bf16[1,1,128,512]{3,2,1,0:T(8,128)(2,1)S(1)}, bf16[1,1,128,512]{3,2,1,0:T(8,128)(2,1)}, u32[]{:S(2)}) copy-start(bf16[1,1,128,512]{3,2,1,0:T(8,128)(2,1)} %param.10) | copy-start | bytes 393220
  7.2 18.4 %copy-start.24 = (bf16[1,1,128,2048]{3,2,1,0:T(8,128)(2,1)S(1)}, bf16[1,1,128,2048]{3,2,1,0:T(8,128)(2,1)}, u32[]{:S(2)}) copy-start(bf16[1,1,128,2048]{3,2,1,0:T(8,128)(2,1)} %param.8) | copy-start | bytes 1572868
  9.9 95.7 %all-to-all-start = ((bf16[16,50,512]{2,1,0:T(8,128)(2,1)}), bf16[16,50,512]{2,1,0:T(8,128)(2,1)S(1)}, u32[]{:S(2)}, u32[]{:S(2)}) async-start(bf16[16,50,512]{2,1,0:T(8,128)(2,1)} %stack.5), calls=%async_computation | async-start | bytes 1835008 | tf_op jit(solution)/shard_map/all_to_all | solution.py:84
  25.3 617.9 %all-reduce.7.cloned.1.call-start = ((), (), s32[]{:S(2)}) async-start(), calls=%async_computation.1 | async-start | bytes 524288 | tf_op jit(solution)/shard_map/psum | solution.py:128
  99.0 3.3 copy-start.15
  99.0 3.3 copy-start.17
  99.0 3.3 copy-start.19
  99.0 5.0 copy-start.21
  104.0 1.9 copy-start.14
  105.6 0.9 copy-start.30
  105.6 1.0 copy-start.33
  106.6 3.7 copy-start.22
  110.3 2.1 copy-start.4
  114.2 1.0 copy-start.31
  114.2 1.4 copy-start.28
  115.6 30.4 %copy-start.10 = (f32[928,128]{1,0:T(8,128)}, f32[928,128]{1,0:T(8,128)S(1)}, u32[]{:S(2)}) copy-start(f32[928,128]{1,0:T(8,128)S(1)} %fusion.19) | copy-start | bytes 1425412
  115.6 3.8 copy-start.20
  119.4 2.9 copy-start.3
  122.3 2.9 copy-start.29
  124.1 2.2 copy-start.26
  126.3 3.7 copy-start.18
  130.0 2.9 copy-start.2
  134.7 1.0 copy-start.27
  134.7 2.2 copy-start.25
  134.7 2.2 copy-start.34
  136.9 3.6 copy-start.16
  140.5 2.1 copy-start.1
  142.6 3.5 copy-start.9
  144.6 1.4 copy-start.11
  144.6 1.4 copy-start.12
  145.6 1.1 copy-start.5
  145.6 1.2 copy-start.7
  221.5 43.0 %copy-start.6 = (f32[928,128]{1,0:T(8,128)S(1)}, f32[928,128]{1,0:T(8,128)}, u32[]{:S(2)}) copy-start(f32[928,128]{1,0:T(8,128)} %convolution_bitcast_fusion.1) | copy-start | bytes 1425412
  221.5 43.0 %copy-start.8 = (f32[928,128]{1,0:T(8,128)S(1)}, f32[928,128]{1,0:T(8,128)}, u32[]{:S(2)}) copy-start(f32[928,128]{1,0:T(8,128)} %convolution_bitcast_fusion.3) | copy-start | bytes 1425412
  223.1 43.8 %collective-permute-start = (f32[56,512]{1,0:T(8,128)}, f32[56,512]{1,0:T(8,128)}, u32[]{:S(2)}, u32[]{:S(2)}) collective-permute-start(f32[56,512]{1,0:T(8,128)} %get-tuple-element.7), channel_id=1, source_target_pairs={{0,1},{1,2},{2,3},{3,4},{4,5},{5,6},{6,7},{7,8},{8,9},{9,10},{10,1... | collective-permute-start | bytes 344072
  225.8 44.6 %collective-permute-start.2 = (f32[56,512]{1,0:T(8,128)S(1)}, f32[56,512]{1,0:T(8,128)}, u32[]{:S(2)}, u32[]{:S(2)}) collective-permute-start(f32[56,512]{1,0:T(8,128)S(1)} %get-tuple-element.8), channel_id=1, source_target_pairs={{0,1},{1,2},{2,3},{3,4},{4,5},{5,6},{6,7},{7,8},{8,9},{9,10},{10,1... | collective-permute-start | bytes 344072
  229.8 37.1 %copy-start.23 = (f32[56,512]{1,0:T(8,128)S(1)}, f32[56,512]{1,0:T(8,128)}, u32[]{:S(2)}) copy-start(f32[56,512]{1,0:T(8,128)} %get-tuple-element.7) | copy-start | bytes 344068
  231.9 38.6 %collective-permute-start.3 = (f32[34,512]{1,0:T(8,128)}, f32[34,512]{1,0:T(8,128)}, u32[]{:S(2)}, u32[]{:S(2)}) collective-permute-start(f32[34,512]{1,0:T(8,128)} %slice.107), channel_id=1, source_target_pairs={{0,2},{1,3},{2,4},{3,5},{4,6},{5,7},{6,8},{7,9},{8,10},{9,11},{10,... | collective-permute-start | bytes 208904
  244.5 21.7 %collective-permute-start.1 = (f32[34,512]{1,0:T(8,128)}, f32[34,512]{1,0:T(8,128)S(1)}, u32[]{:S(2)}, u32[]{:S(2)}) collective-permute-start(f32[34,512]{1,0:T(8,128)} %slice.106), channel_id=1, source_target_pairs={{0,2},{1,3},{2,4},{3,5},{4,6},{5,7},{6,8},{7,9},{8,10},{9,11},{10,... | collective-permute-start | bytes 208904
  265.4 8.7 %copy-start.32 = (bf16[4096,16]{0,1:T(8,128)(2,1)S(1)}, bf16[4096,16]{0,1:T(8,128)(2,1)}, u32[]{:S(2)}) copy-start(bf16[4096,16]{0,1:T(8,128)(2,1)} %param.13) | copy-start | bytes 393220
  266.2 0.6 copy-start.35
  268.9 108.9 %copy-start.36 = (bf16[16,512]{1,0:T(8,128)(2,1)S(1)}, bf16[16,512]{1,0:T(8,128)(2,1)}, u32[]{:S(2)}) copy-start(bf16[16,512]{1,0:T(8,128)(2,1)} %param.14) | copy-start | bytes 49156
Sparse Core Ops, SparseCore 0:
  379.2 263.9 all-reduce.6
